TPU v7x, 32 devices: a whole 2x2x4 slice. The times are simulated.
32 devices in a mesh: fsdp: 8 (over z, y), rows: 4 (over x, core).
Axes of the slice: x: 2, y: 2, z: 4, core: 2. Of those that a mesh axis runs over, the one named last changes fastest.
Arguments:
- frames: bfloat16 [8, 12, 16, 1536], P('fsdp', 'rows'), may hold values from -6 to 6
- kernel: float32 [7, 7, 1536], replicated, may hold values from -0.875 to 0.875
- kernel_bias: float32 [1536], replicated, may hold values from -3 to 3
- layer_norm_weight: float32 [1536], replicated, may hold values from 0.25 to 1.75
- layer_norm_bias: float32 [1536], replicated, may hold values from -3 to 3
- up_weight: bfloat16 [1536, 6144], P('fsdp', 'rows'), may hold values from -1 to 1, as said below
- up_bias: float32 [6144], P('rows'), may hold values from -3 to 3
- grn_gamma: float32 [6144], P('rows'), may hold values from 0.2 to 1
- grn_beta: float32 [6144], P('rows'), may hold values from -3 to 3
- grad_out: bfloat16 [8, 12, 16, 6144], P('fsdp', None, None, 'rows'), may hold values from -8 to 8, as said below
Outputs:
- activation: bfloat16 [8, 12, 16, 6144], P('fsdp', None, None, 'rows')
- frames_grad: bfloat16 [8, 12, 16, 1536], P('fsdp', 'rows')
- up_weight_grad: float32 [1536, 6144], P('fsdp', 'rows')
- kernel_grad: float32 [7, 7, 1536], replicated
Inputs may be any that keep to these rules, and one draw needn't show every extreme that they name: `up_weight`: entries lie within the bounds. `grad_out`: entries lie within the bounds.
All inputs are finite; a program needn't handle non-finite values.
Results may differ from a plain program's by a relative error of at most 0.014.
Values may be sent and summed in bfloat16 or wider, within the bound.
No kernel may reach another device: no remote copies, remote signals or barrier semaphores. Data moves between devices by JAX's collectives and lax.ppermute only.
A program may use at most 64 MiB of HBM per device.

v0:
```python
import jax
import jax.numpy as jnp
from jax import lax
from jax.sharding import PartitionSpec as P

FF = 6144


def extended(block, sides, width):
    for axis, dim in sides:
        count = lax.axis_size(axis)
        forward = [(i, i + 1) for i in range(count - 1)]
        backward = [(target, source) for source, target in forward]
        low = lax.ppermute(
            lax.slice_in_dim(block, block.shape[dim] - width, None, axis=dim), axis, forward
        )
        high = lax.ppermute(lax.slice_in_dim(block, 0, width, axis=dim), axis, backward)
        block = jnp.concatenate([low, block, high], axis=dim)
    return block


def conv_rows(framed, kern, kbias):
    rows = framed.shape[0] - 6
    cols = framed.shape[1]
    wide = jnp.pad(framed, ((0, 0), (3, 3), (0, 0)))
    total = jnp.zeros((rows, cols, framed.shape[2]), jnp.float32) + kbias
    for i in range(kern.shape[0]):
        for j in range(kern.shape[1]):
            total = total + wide[i : i + rows, j : j + cols].astype(jnp.float32) * kern[i, j]
    return total


def back_conv(grad_pad, kern):
    rows = grad_pad.shape[0] - 6
    cols = grad_pad.shape[1]
    wide = jnp.pad(grad_pad, ((0, 0), (3, 3), (0, 0)))
    total = jnp.zeros((rows, cols, grad_pad.shape[2]), jnp.float32)
    for i in range(kern.shape[0]):
        for j in range(kern.shape[1]):
            total = (
                total
                + wide[6 - i : 6 - i + rows, 6 - j : 6 - j + cols].astype(jnp.float32) * kern[i, j]
            )
    return total


def kern_grad(framed, grad_rows):
    rows = grad_rows.shape[0]
    cols = grad_rows.shape[1]
    wide = jnp.pad(framed, ((0, 0), (3, 3), (0, 0)))
    grad_f = grad_rows.astype(jnp.float32)
    parts = []
    for i in range(7):
        for j in range(7):
            parts.append(
                jnp.sum(wide[i : i + rows, j : j + cols].astype(jnp.float32) * grad_f, axis=(0, 1))
            )
    return jnp.stack(parts).reshape(7, 7, grad_rows.shape[2])


def apply_layer_norm(activation_rows, scale_factor, offset_bias):
    centered_input = activation_rows - jnp.mean(activation_rows, axis=-1, keepdims=True)
    inverse_deviation = lax.rsqrt(
        jnp.mean(centered_input * centered_input, axis=-1, keepdims=True) + 1e-06
    )
    standardized_input = centered_input * inverse_deviation
    return (
        (standardized_input * scale_factor + offset_bias).astype(jnp.bfloat16),
        standardized_input,
        inverse_deviation,
    )


def gelu_grad(value):
    return (
        0.5 * (1.0 + jax.scipy.special.erf(value * 0.7071067811865476))
        + value * jnp.exp(-0.5 * value * value) * 0.3989422804014327
    )


def layer_norm_backward(normed_input_gradient, scale_factor, standardized_input, inverse_deviation):
    scaled_output = normed_input_gradient * scale_factor
    return (
        inverse_deviation
        * (
            scaled_output
            - jnp.mean(scaled_output, axis=-1, keepdims=True)
            - standardized_input
            * jnp.mean(scaled_output * standardized_input, axis=-1, keepdims=True)
        )
    ).astype(jnp.bfloat16)


def body(
    frames,
    kernel,
    kernel_bias,
    layer_norm_weight,
    layer_norm_bias,
    up_weight,
    up_bias,
    grn_gamma,
    grn_beta,
    grad_out,
):
    slab = frames[0]
    chans = slab.shape[2]
    columns = lax.all_gather(up_weight, "fsdp", axis=0, tiled=True)
    padded = extended(slab, (("rows", 0),), 3)
    activation_rows = conv_rows(padded, kernel, kernel_bias)
    normed_output, standardized_input, inverse_deviation = apply_layer_norm(
        activation_rows, layer_norm_weight, layer_norm_bias
    )
    whole = lax.all_gather(normed_output, "rows", axis=0, tiled=True)
    height = whole.shape[0]
    cols = whole.shape[1]
    flat = whole.reshape(-1, chans)
    pre = jnp.dot(flat, columns, preferred_element_type=jnp.float32) + up_bias
    post = jax.nn.gelu(pre, approximate=False)
    norms = jnp.sqrt(jnp.sum(post * post, axis=0) + 1e-06)
    cot_f = grad_out[0].reshape(flat.shape[0], -1).astype(jnp.float32)
    dnorm = grn_gamma * jnp.sum(cot_f * post, axis=0)
    norm_total = lax.psum(jnp.sum(norms), "rows")
    denom = norm_total / FF + 1e-06
    ratio = norms / denom
    output = (grn_gamma * (post * ratio) + grn_beta + post).astype(jnp.bfloat16)
    cross = lax.psum(jnp.sum(dnorm * norms), "rows")
    dnorms = dnorm / denom - cross / (denom * denom) / FF
    dpost = cot_f * (1.0 + grn_gamma * ratio) + post * (dnorms / norms)
    dpre = (dpost * gelu_grad(pre)).astype(jnp.bfloat16)
    w_term = lax.dot_general(
        flat, dpre, (((0,), (0,)), ((), ())), preferred_element_type=jnp.float32
    )
    up_grad = lax.psum_scatter(
        w_term.astype(jnp.bfloat16), "fsdp", scatter_dimension=0, tiled=True
    ).astype(jnp.float32)
    dpre_rows = dpre.reshape(height, cols, -1)
    normed_input_gradient = lax.psum_scatter(
        jnp.einsum("hwf,cf->hwc", dpre_rows, columns, preferred_element_type=jnp.float32).astype(
            jnp.bfloat16
        ),
        "rows",
        scatter_dimension=0,
        tiled=True,
    ).astype(jnp.float32)
    activation_gradient = layer_norm_backward(
        normed_input_gradient, layer_norm_weight, standardized_input, inverse_deviation
    )
    grad_pad = extended(activation_gradient, (("rows", 0),), 3)
    dframe = back_conv(grad_pad, kernel).astype(jnp.bfloat16)
    kernel_local = kern_grad(padded, activation_gradient)
    kernel_total = lax.psum(kernel_local, ("fsdp", "rows"))
    activation = output.reshape(1, height, cols, -1)
    return (activation, dframe.reshape((1,) + dframe.shape), up_grad, kernel_total)


def solution(mesh):
    placed = (
        P("fsdp", "rows", None, None),
        P(),
        P(),
        P(),
        P(),
        P("fsdp", "rows"),
        P("rows"),
        P("rows"),
        P("rows"),
        P("fsdp", None, None, "rows"),
    )
    return jax.shard_map(
        body,
        mesh=mesh,
        in_specs=placed,
        out_specs=(
            P("fsdp", None, None, "rows"),
            P("fsdp", "rows", None, None),
            P("fsdp", "rows"),
            P(),
        ),
        check_vma=False,
    )
```

profile of v0, /device:TPU:1, one launch (start us, length us, event | category | flops | bytes accessed | tf_op | source)
XLA Modules:
  0.0 376.6 jit_solution(9324311914852352310)
XLA Ops:
  7.2 0.0 all-gather.2.cloned.1.call-start
  7.2 0.7 all-gather.2.cloned.1.call-update
  7.9 0.0 reduce-scatter.3.cloned.1.call-start
  8.0 2.0 collective-permute-start.1
  9.9 4.5 %collective-permute-start = (bf16[3,16,1536]{2,1,0:T(8,128)(2,1)}, bf16[3,16,1536]{2,1,0:T(8,128)(2,1)S(1)}, u32[]{:S(2)}, u32[]{:S(2)}) collective-permute-start(bf16[3,16,1536]{2,1,0:T(8,128)(2,1)} %bitcast.25), channel_id=1, source_target_pairs={{0,1},{1,2},{2,3},{4,5},{5,6},{6,7},{8,9},{9,10},{10,11},{12,13},{... | collective-permute-start | bytes 442376 | tf_op jit(solution)/shard_map/ppermute | solution.py:14
  14.4 2.0 slice_reduce_fusion.48
  16.4 1.3 slice_reduce_fusion.46
  17.7 0.0 copy-start.4
  17.7 1.8 slice_reduce_fusion.47
  19.7 0.0 collective-permute-done.1
  19.7 0.0 collective-permute-done
  19.7 0.0 copy-done
  19.7 0.2 select_maximum_fusion.2
  20.0 0.0 copy-start.3
  20.0 0.0 copy-start.50
  20.0 3.4 fusion.158
  23.4 0.0 copy-done.6
  23.4 0.0 copy-done.12
  23.4 0.0 copy-done.14
  23.4 0.0 copy-done.16
  23.5 0.0 copy-done.18
  23.5 0.0 copy-done.20
  23.5 0.0 copy-done.22
  23.5 0.0 copy-done.24
  23.5 0.0 copy-done.26
  23.5 0.0 copy-done.28
  23.5 0.0 copy-done.30
  23.6 0.0 copy-start.1
  23.6 0.0 copy-start.53
  23.6 0.2 multiply_reduce_fusion.2
  23.8 0.4 copy-done.46
  24.2 0.6 copy-done.48
  24.8 0.1 add_convert_fusion.1
  24.9 6.9 %all_gather.6 = bf16[12,16,1536]{2,1,0:T(8,128)(2,1)S(1)} all-gather(bf16[3,16,1536]{2,1,0:T(8,128)(2,1)S(1)} %add_convert_fusion.1), channel_id=1, replica_groups=mesh['fsdp'=8,'rows'=4] {'rows'}, dimensions={0}, use_global_device_ids=true | all-gather | bytes 737280 | tf_op jit(solution)/shard_map/all_gather | solution.py:114
  31.8 59.4 %all-gather.2.cloned.1.call-done = bf16[1536,1536]{1,0:T(8,128)(2,1)} async-done(((bf16[192,1536]{1,0:T(8,128)(2,1)}), bf16[1536,1536]{1,0:T(8,128)(2,1)}) %all-gather.2.cloned.1.call-update) | async-done | bytes 4718608 | tf_op jit(solution)/shard_map/all_gather | solution.py:108
  91.2 7.3 %fusion.9 = (f32[1536]{0:T(1024)S(1)}, f32[1536]{0:T(1024)S(1)}, f32[192,1536]{1,0:T(8,128)}, f32[192,1536]{1,0:T(8,128)}) fusion(bf16[1,12,16,1536]{3,2,1,0:T(8,128)(2,1)S(1)} %copy-done.1, f32[1536]{0:T(1024)S(1)} %copy-done.53, bf16[192,1536]{1,0:T(8,128)(2,1)S(1)} %bitcast.21, bf16[1536,1536]{1,0:T(8,128)(2,1)} %all-gather.2.cloned.1.call-done), kind=kOutput, calls=%fused_computation.65 | convolution fusion | flops 926610432 | bytes 8275968 | tf_op jit(solution)/shard_map/dot_general | solution.py:118
  98.6 0.7 multiply_reduce_fusion.3
  99.2 7.3 %all-reduce.2 = (f32[]{:T(128)}, f32[]{:T(128)}) all-reduce(f32[]{:T(128)} %get-tuple-element.115, f32[]{:T(128)} %get-tuple-element.114), channel_id=1, replica_groups=mesh['fsdp'=8,'rows'=4] {'rows'}, use_global_device_ids=true, to_apply=%region_4.5 | all-reduce | flops 2 | bytes 16 | tf_op jit(solution)/shard_map/psum | solution.py:123
  107.9 3.2 fusion.8
  111.1 4.8 %fusion.2 = bf16[12,16,1536]{2,1,0:T(8,128)(2,1)} fusion(bf16[12,16,1536]{2,1,0:T(8,128)(2,1)S(1)} %bitcast.23, bf16[1536,1536]{1,0:T(8,128)(2,1)} %all-gather.2.cloned.1.call-done), kind=kOutput, calls=%fused_computation.54 | convolution fusion | flops 906264576 | bytes 5898240 | tf_op jit(solution)/shard_map/hwf,cf->hwc/dot_general | solution.py:139
  116.0 0.0 reduce-scatter.3.cloned.1.call-update
  116.0 0.0 reduce-scatter.5.cloned.1.call-start
  116.0 3.6 convolution_convert_fusion
  119.6 0.0 reduce-scatter.5.cloned.1.call-update
  119.6 0.0 all-reduce.5.cloned.1.call-start
  119.7 16.9 %reduce-scatter.3.cloned.1.call-done = bf16[3,16,1536]{2,1,0:T(8,128)(2,1)} async-done(((bf16[12,16,1536]{2,1,0:T(8,128)(2,1)}), bf16[3,16,1536]{2,1,0:T(8,128)(2,1)}) %reduce-scatter.3.cloned.1.call-update) | async-done | bytes 147472 | tf_op jit(solution)/shard_map/reduce_scatter | solution.py:138
  136.6 1.1 fusion.147
  137.7 1.9 fusion.145
  139.6 2.8 collective-permute-start.3
  142.3 3.0 collective-permute-start.2
  145.3 0.8 fusion.146
  146.1 0.6 fusion.136
  147.4 0.5 stack.199
  147.9 0.0 copy-start.5
  148.1 0.8 reshape.62
  148.9 0.0 all-reduce.5.cloned.1.call-update
  148.9 0.0 collective-permute-done.3
  148.9 0.0 collective-permute-done.2
  148.9 0.2 select_maximum_fusion
  149.3 2.8 fusion.153
  152.1 83.8 %reduce-scatter.5.cloned.1.call-done = bf16[192,1536]{1,0:T(8,128)(2,1)} async-done(((bf16[1536,1536]{1,0:T(8,128)(2,1)}), bf16[192,1536]{1,0:T(8,128)(2,1)}) %reduce-scatter.5.cloned.1.call-update) | async-done | bytes 589840 | tf_op jit(solution)/shard_map/reduce_scatter | solution.py:134
  235.9 2.2 convert_element_type.489
  238.1 130.2 %all-reduce.5.cloned.1.call-done = f32[7,7,1536]{2,1,0:T(8,128)} async-done(((f32[7,7,1536]{2,1,0:T(8,128)}), f32[7,7,1536]{2,1,0:T(8,128)}) %all-reduce.5.cloned.1.call-update) | async-done | bytes 301072 | tf_op jit(solution)/shard_map/psum | solution.py:152
  368.3 1.7 copy.15
  (141 shorter events, 0.5 us)
Async XLA Ops:
  7.2 12.6 %copy-start = (bf16[1,3,16,1536]{3,2,1,0:T(8,128)(2,1)S(1)}, bf16[1,3,16,1536]{3,2,1,0:T(8,128)(2,1)}, u32[]{:S(2)}) copy-start(bf16[1,3,16,1536]{3,2,1,0:T(8,128)(2,1)} %param.10) | copy-start | bytes 442372
  7.2 12.8 %copy-start.52 = (f32[1536]{0:T(1024)S(1)}, f32[1536]{0:T(1024)}, u32[]{:S(2)}) copy-start(f32[1536]{0:T(1024)} %param.12) | copy-start | bytes 18436
  7.2 84.0 %all-gather.2.cloned.1.call-start = ((), (), s32[]{:S(2)}) async-start(), calls=%async_computation.2 | async-start | bytes 5308416 | tf_op jit(solution)/shard_map/all_gather | solution.py:108
  7.9 128.7 %reduce-scatter.3.cloned.1.call-start = ((), (), s32[]{:S(2)}) async-start(), calls=%async_computation.3 | async-start | bytes 737280 | tf_op jit(solution)/shard_map/reduce_scatter | solution.py:138
  8.0 11.7 %collective-permute-start.1 = (bf16[3,16,1536]{2,1,0:T(8,128)(2,1)}, bf16[3,16,1536]{2,1,0:T(8,128)(2,1)S(1)}, u32[]{:S(2)}, u32[]{:S(2)}) collective-permute-start(bf16[3,16,1536]{2,1,0:T(8,128)(2,1)} %bitcast.24), channel_id=1, source_target_pairs={{1,0},{2,1},{3,2},{5,4},{6,5},{7,6},{9,8},{10,9},{11,10},{13,12},{... | collective-permute-start | bytes 442376 | tf_op jit(solution)/shard_map/ppermute | solution.py:17
  9.9 9.8 %collective-permute-start = (bf16[3,16,1536]{2,1,0:T(8,128)(2,1)}, bf16[3,16,1536]{2,1,0:T(8,128)(2,1)S(1)}, u32[]{:S(2)}, u32[]{:S(2)}) collective-permute-start(bf16[3,16,1536]{2,1,0:T(8,128)(2,1)} %bitcast.25), channel_id=1, source_target_pairs={{0,1},{1,2},{2,3},{4,5},{5,6},{6,7},{8,9},{9,10},{10,11},{12,13},{... | collective-permute-start | bytes 442376 | tf_op jit(solution)/shard_map/ppermute | solution.py:14
  17.7 5.7 %copy-start.4 = (f32[1536]{0:T(1024)}, f32[1536]{0:T(1024)S(1)}, u32[]{:S(2)}) copy-start(f32[1536]{0:T(1024)S(1)} %get-tuple-element.99) | copy-start | bytes 18436
  17.7 5.7 %copy-start.6 = (f32[1536]{0:T(1024)}, f32[1536]{0:T(1024)S(1)}, u32[]{:S(2)}) copy-start(f32[1536]{0:T(1024)S(1)} %get-tuple-element.100) | copy-start | bytes 18436
  19.5 3.9 %copy-start.8 = (f32[1536]{0:T(1024)}, f32[1536]{0:T(1024)S(1)}, u32[]{:S(2)}) copy-start(f32[1536]{0:T(1024)S(1)} %get-tuple-element.71) | copy-start | bytes 18436
  19.5 3.9 %copy-start.10 = (f32[1536]{0:T(1024)}, f32[1536]{0:T(1024)S(1)}, u32[]{:S(2)}) copy-start(f32[1536]{0:T(1024)S(1)} %get-tuple-element.72) | copy-start | bytes 18436
  19.5 3.9 %copy-start.12 = (f32[1536]{0:T(1024)}, f32[1536]{0:T(1024)S(1)}, u32[]{:S(2)}) copy-start(f32[1536]{0:T(1024)S(1)} %get-tuple-element.73) | copy-start | bytes 18436
  19.5 3.9 %copy-start.14 = (f32[1536]{0:T(1024)}, f32[1536]{0:T(1024)S(1)}, u32[]{:S(2)}) copy-start(f32[1536]{0:T(1024)S(1)} %get-tuple-element.74) | copy-start | bytes 18436
  19.5 3.9 %copy-start.16 = (f32[1536]{0:T(1024)}, f32[1536]{0:T(1024)S(1)}, u32[]{:S(2)}) copy-start(f32[1536]{0:T(1024)S(1)} %get-tuple-element.75) | copy-start | bytes 18436
  19.6 3.9 %copy-start.18 = (f32[1536]{0:T(1024)}, f32[1536]{0:T(1024)S(1)}, u32[]{:S(2)}) copy-start(f32[1536]{0:T(1024)S(1)} %get-tuple-element.76) | copy-start | bytes 18436
  19.6 3.9 %copy-start.20 = (f32[1536]{0:T(1024)}, f32[1536]{0:T(1024)S(1)}, u32[]{:S(2)}) copy-start(f32[1536]{0:T(1024)S(1)} %get-tuple-element.77) | copy-start | bytes 18436
  19.6 3.9 %copy-start.22 = (f32[1536]{0:T(1024)}, f32[1536]{0:T(1024)S(1)}, u32[]{:S(2)}) copy-start(f32[1536]{0:T(1024)S(1)} %get-tuple-element.78) | copy-start | bytes 18436
  19.6 3.9 %copy-start.24 = (f32[1536]{0:T(1024)}, f32[1536]{0:T(1024)S(1)}, u32[]{:S(2)}) copy-start(f32[1536]{0:T(1024)S(1)} %get-tuple-element.79) | copy-start | bytes 18436
  19.6 3.9 %copy-start.26 = (f32[1536]{0:T(1024)}, f32[1536]{0:T(1024)S(1)}, u32[]{:S(2)}) copy-start(f32[1536]{0:T(1024)S(1)} %get-tuple-element.80) | copy-start | bytes 18436
  19.6 3.9 %copy-start.28 = (f32[1536]{0:T(1024)}, f32[1536]{0:T(1024)S(1)}, u32[]{:S(2)}) copy-start(f32[1536]{0:T(1024)S(1)} %get-tuple-element.81) | copy-start | bytes 18436
  19.6 3.9 %copy-start.30 = (f32[1536]{0:T(1024)}, f32[1536]{0:T(1024)S(1)}, u32[]{:S(2)}) copy-start(f32[1536]{0:T(1024)S(1)} %get-tuple-element.82) | copy-start | bytes 18436
  19.6 3.9 %copy-start.32 = (f32[1536]{0:T(1024)}, f32[1536]{0:T(1024)S(1)}, u32[]{:S(2)}) copy-start(f32[1536]{0:T(1024)S(1)} %get-tuple-element.83) | copy-start | bytes 18436
  19.6 3.9 %copy-start.34 = (f32[1536]{0:T(1024)}, f32[1536]{0:T(1024)S(1)}, u32[]{:S(2)}) copy-start(f32[1536]{0:T(1024)S(1)} %get-tuple-element.84) | copy-start | bytes 18436
  19.6 3.9 %copy-start.36 = (f32[1536]{0:T(1024)}, f32[1536]{0:T(1024)S(1)}, u32[]{:S(2)}) copy-start(f32[1536]{0:T(1024)S(1)} %get-tuple-element.85) | copy-start | bytes 18436
  19.7 3.9 %copy-start.38 = (f32[1536]{0:T(1024)}, f32[1536]{0:T(1024)S(1)}, u32[]{:S(2)}) copy-start(f32[1536]{0:T(1024)S(1)} %get-tuple-element.86) | copy-start | bytes 18436
  19.7 3.9 %copy-start.40 = (f32[1536]{0:T(1024)}, f32[1536]{0:T(1024)S(1)}, u32[]{:S(2)}) copy-start(f32[1536]{0:T(1024)S(1)} %get-tuple-element.87) | copy-start | bytes 18436
  19.7 3.9 %copy-start.42 = (f32[1536]{0:T(1024)}, f32[1536]{0:T(1024)S(1)}, u32[]{:S(2)}) copy-start(f32[1536]{0:T(1024)S(1)} %get-tuple-element.88) | copy-start | bytes 18436
  19.7 3.9 %copy-start.44 = (f32[1536]{0:T(1024)}, f32[1536]{0:T(1024)S(1)}, u32[]{:S(2)}) copy-start(f32[1536]{0:T(1024)S(1)} %get-tuple-element.89) | copy-start | bytes 18436
  20.0 4.8 %copy-start.3 = (f32[1536]{0:T(1024)S(1)}, f32[1536]{0:T(1024)}, u32[]{:S(2)}) copy-start(f32[1536]{0:T(1024)} %param.13) | copy-start | bytes 18436
  20.0 4.8 %copy-start.50 = (f32[1536]{0:T(1024)S(1)}, f32[1536]{0:T(1024)}, u32[]{:S(2)}) copy-start(f32[1536]{0:T(1024)} %param.14) | copy-start | bytes 18436
  23.6 67.6 %copy-start.1 = (bf16[1,12,16,1536]{3,2,1,0:T(8,128)(2,1)S(1)}, bf16[1,12,16,1536]{3,2,1,0:T(8,128)(2,1)}, u32[]{:S(2)}) copy-start(bf16[1,12,16,1536]{3,2,1,0:T(8,128)(2,1)} %param.19) | copy-start | bytes 1769476
  23.6 67.6 %copy-start.53 = (f32[1536]{0:T(1024)S(1)}, f32[1536]{0:T(1024)}, u32[]{:S(2)}) copy-start(f32[1536]{0:T(1024)} %param.16) | copy-start | bytes 18436
  23.6 0.6 copy-start.46
  24.2 0.6 copy-start.48
  91.2 7.4 %copy-start.2 = (f32[1536]{0:T(1024)S(1)}, f32[1536]{0:T(1024)}, u32[]{:S(2)}) copy-start(f32[1536]{0:T(1024)} %param.17) | copy-start | bytes 18436
  91.2 16.7 %copy-start.51 = (f32[1536]{0:T(1024)S(1)}, f32[1536]{0:T(1024)}, u32[]{:S(2)}) copy-start(f32[1536]{0:T(1024)} %param.18) | copy-start | bytes 18436
  116.0 119.9 %reduce-scatter.5.cloned.1.call-start = ((), (), s32[]{:S(2)}) async-start(), calls=%async_computation.4 | async-start | bytes 5308416 | tf_op jit(solution)/shard_map/reduce_scatter | solution.py:134
  119.6 17.0 %copy-start.47 = (f32[3,16]{1,0:T(4,128)S(1)}, f32[3,16]{1,0:T(4,128)}, u32[]{:S(2)}) copy-start(f32[3,16]{1,0:T(4,128)} %copy-done.46) | copy-start | bytes 580
  119.6 17.0 %copy-start.49 = (f32[3,16]{1,0:T(4,128)S(1)}, f32[3,16]{1,0:T(4,128)}, u32[]{:S(2)}) copy-start(f32[3,16]{1,0:T(4,128)} %copy-done.48) | copy-start | bytes 580
  119.6 248.7 %all-reduce.5.cloned.1.call-start = ((), (), s32[]{:S(2)}) async-start(), calls=%async_computation.5 | async-start | bytes 688128 | tf_op jit(solution)/shard_map/psum | solution.py:152
  139.6 9.3 %collective-permute-start.3 = (bf16[3,16,1536]{2,1,0:T(8,128)(2,1)S(1)}, bf16[3,16,1536]{2,1,0:T(8,128)(2,1)S(1)}, u32[]{:S(2)}, u32[]{:S(2)}) collective-permute-start(bf16[3,16,1536]{2,1,0:T(8,128)(2,1)S(1)} %get-tuple-element.118), channel_id=1, source_target_pairs={{1,0},{2,1},{3,2},{5,4},{6,5},{7,6},{9,8},{10,9},{11,10},{13,12},{... | collective-permute-start | bytes 442376 | tf_op jit(solution)/shard_map/ppermute | solution.py:17
  142.3 6.6 %collective-permute-start.2 = (bf16[3,16,1536]{2,1,0:T(8,128)(2,1)S(1)}, bf16[3,16,1536]{2,1,0:T(8,128)(2,1)S(1)}, u32[]{:S(2)}, u32[]{:S(2)}) collective-permute-start(bf16[3,16,1536]{2,1,0:T(8,128)(2,1)S(1)} %get-tuple-element.118), channel_id=1, source_target_pairs={{0,1},{1,2},{2,3},{4,5},{5,6},{6,7},{8,9},{9,10},{10,11},{12,13},{... | collective-permute-start | bytes 442376 | tf_op jit(solution)/shard_map/ppermute | solution.py:14
  147.9 1.3 copy-start.5
  147.9 1.3 copy-start.7
  147.9 1.3 copy-start.9
  147.9 1.3 copy-start.11
  147.9 1.3 copy-start.13
  147.9 1.3 copy-start.15
  147.9 1.3 copy-start.17
  147.9 1.3 copy-start.19
  148.0 1.3 copy-start.21
  148.0 1.3 copy-start.23
  148.0 1.3 copy-start.25
  148.0 1.3 copy-start.27
  148.0 1.3 copy-start.29
  148.0 1.3 copy-start.31
  148.0 1.3 copy-start.33
  148.0 1.3 copy-start.35
  148.0 1.3 copy-start.37
  148.0 1.3 copy-start.39
  148.1 1.3 copy-start.41
  148.1 1.3 copy-start.43
  148.1 1.3 copy-start.45
Sparse Core Ops, SparseCore 0:
  10.2 80.9 all-gather.1
  116.1 20.4 reduce-scatter.2
  140.3 95.5 reduce-scatter.4
  241.7 126.5 all-reduce.4
where the time goes:
time: 377 us
  waiting for transfers between devices  291 us (77%)
  other arithmetic  17.4 us (5%)
  between operations  16.3 us (4%)
  matrix products  15.7 us (4%)
  blocking collectives  14.2 us (4%)
  starting transfers between devices  12.3 us (3%)
  local copies, waits for them, and re-layouts  9.57 us (3%)
    psum x1, waiting for transfers between devices, body(): kernel_total = lax.psum(kernel_local, ('fsdp', 'rows'))  130 us
    reduce_scatter x1, waiting for transfers between devices, body(): lax.psum_scatter(w_term.astype(jnp.bfloat16), 'fsdp', scatter_dimension=0...  83.8 us
    all_gather x1, waiting for transfers between devices, body(): columns = lax.all_gather(up_weight, 'fsdp', axis=0, tiled=True)  59.4 us
    reduce_scatter x1, waiting for transfers between devices, body(): lax.psum_scatter(jnp.einsum('hwf,cf->hwc', dpre_rows, columns, preferred_...  16.9 us
  transfers between devices with their start and end apart: 8, of which 4 were waited for; matrix products, arithmetic and copies ran while one was open for 6% of the time, Pallas kernels for 0%

commit v1 on v0

--- a/solution.py
+++ b/solution.py
@@ -105,7 +105,12 @@
 ):
     slab = frames[0]
     chans = slab.shape[2]
-    columns = lax.all_gather(up_weight, "fsdp", axis=0, tiled=True)
+    ring = [up_weight]
+    for hop in range(7):
+        ring.append(lax.ppermute(ring[-1], "fsdp", [(dev, (dev + 1) % 8) for dev in range(8)]))
+    columns = jnp.roll(
+        jnp.concatenate(ring[::-1], axis=0), (lax.axis_index("fsdp") + 1) * ring[0].shape[0], axis=0
+    )
     padded = extended(slab, (("rows", 0),), 3)
     activation_rows = conv_rows(padded, kernel, kernel_bias)
     normed_output, standardized_input, inverse_deviation = apply_layer_norm(

time: 377 us -> 404 us (1.072)
  blocking collectives: 14.2 us -> 24 us
  waiting for transfers between devices: 291 us -> 298 us
  local copies, waits for them, and re-layouts: 9.57 us -> 15.1 us
    ppermute x0 -> x7, waiting for transfers between devices: none -> 69.5 us  [body(): lax.ppermute(ring[-1], 'fsdp', [(dev, (dev + 1) % 8) for dev in range(8)])]
    all_gather x1 -> x0, waiting for transfers between devices: 59.4 us -> none  [body(): columns = lax.all_gather(up_weight, 'fsdp', axis=0, tiled=True)]
    all_gather x1, blocking collectives: 6.86 us -> 12.4 us  [body(): whole = lax.all_gather(normed_output, 'rows', axis=0, tiled=True)]
    unnamed x109 -> x218, local copies, waits for them, and re-layouts: 2.91 us -> 7.55 us
    psum x1, blocking collectives: 7.32 us -> 11.6 us  [body(): norm_total = lax.psum(jnp.sum(norms), 'rows')]
  transfers between devices with their start and end apart: 8 -> 14, of which waited for: 4 -> 9; matrix products, arithmetic and copies ran while one was open for 6% -> 6% of each run, Pallas kernels for 0% -> 0%
where the time goes in v1:
time: 404 us; the launch traced here: 403 us
  waiting for transfers between devices  298 us (74%)
  blocking collectives  24 us (6%)
  other arithmetic  18.9 us (5%)
  between operations  17.1 us (4%)
  starting transfers between devices  15.8 us (4%)
  local copies, waits for them, and re-layouts  15.1 us (4%)
  matrix products  13.6 us (3%)
    psum x1, waiting for transfers between devices, body(): kernel_total = lax.psum(kernel_local, ('fsdp', 'rows'))  130 us
    reduce_scatter x1, waiting for transfers between devices, body(): lax.psum_scatter(w_term.astype(jnp.bfloat16), 'fsdp', scatter_dimension=0...  83.4 us
    ppermute x7, waiting for transfers between devices, body(): lax.ppermute(ring[-1], 'fsdp', [(dev, (dev + 1) % 8) for dev in range(8)])  69.5 us
    reduce_scatter x1, waiting for transfers between devices, body(): lax.psum_scatter(jnp.einsum('hwf,cf->hwc', dpre_rows, columns, preferred_...  14.8 us
    all_gather x1, blocking collectives, body(): whole = lax.all_gather(normed_output, 'rows', axis=0, tiled=True)  12.4 us
    psum x1, blocking collectives, body(): norm_total = lax.psum(jnp.sum(norms), 'rows')  11.6 us
    ppermute x2, starting transfers between devices, extended(): lax.ppermute(lax.slice_in_dim(block, block.shape[dim] - width, None, axis...  8.68 us
  transfers between devices with their start and end apart: 14, of which 9 were waited for; matrix products, arithmetic and copies ran while one was open for 6% of the time, Pallas kernels for 0%

profile of v1, /device:TPU:1, one launch (start us, length us, event | category | flops | bytes accessed | tf_op | source)
XLA Modules:
  0.0 402.6 jit_solution(4147718608542229416)
XLA Ops:
  7.2 0.0 copy-start.3
  7.2 0.0 reduce-scatter.3.cloned.1.call-start
  7.2 2.1 collective-permute-start.2
  9.3 16.3 %collective-permute-done.2 = bf16[192,1536]{1,0:T(8,128)(2,1)S(1)} collective-permute-done((bf16[192,1536]{1,0:T(8,128)(2,1)}, bf16[192,1536]{1,0:T(8,128)(2,1)S(1)}, u32[]{:S(2)}, u32[]{:S(2)}) %collective-permute-start.2) | collective-permute-done | bytes 589856 | tf_op jit(solution)/shard_map/ppermute | solution.py:110
  25.6 0.0 collective-permute-start.3
  25.7 16.3 %collective-permute-done.3 = bf16[192,1536]{1,0:T(8,128)(2,1)S(1)} collective-permute-done((bf16[192,1536]{1,0:T(8,128)(2,1)S(1)}, bf16[192,1536]{1,0:T(8,128)(2,1)S(1)}, u32[]{:S(2)}, u32[]{:S(2)}) %collective-permute-start.3) | collective-permute-done | bytes 589856 | tf_op jit(solution)/shard_map/ppermute | solution.py:110
  41.9 15.4 %collective-permute-done.4 = bf16[192,1536]{1,0:T(8,128)(2,1)S(1)} collective-permute-done((bf16[192,1536]{1,0:T(8,128)(2,1)S(1)}, bf16[192,1536]{1,0:T(8,128)(2,1)S(1)}, u32[]{:S(2)}, u32[]{:S(2)}) %collective-permute-start.4) | collective-permute-done | bytes 589856 | tf_op jit(solution)/shard_map/ppermute | solution.py:110
  57.3 5.7 %collective-permute-start = (bf16[3,16,1536]{2,1,0:T(8,128)(2,1)}, bf16[3,16,1536]{2,1,0:T(8,128)(2,1)S(1)}, u32[]{:S(2)}, u32[]{:S(2)}) collective-permute-start(bf16[3,16,1536]{2,1,0:T(8,128)(2,1)} %bitcast.23), channel_id=1, source_target_pairs={{0,1},{1,2},{2,3},{4,5},{5,6},{6,7},{8,9},{9,10},{10,11},{12,13},{... | collective-permute-start | bytes 442376 | tf_op jit(solution)/shard_map/ppermute | solution.py:14
  63.0 1.9 collective-permute-start.1
  65.0 6.8 %collective-permute-done.5 = bf16[192,1536]{1,0:T(8,128)(2,1)S(1)} collective-permute-done((bf16[192,1536]{1,0:T(8,128)(2,1)S(1)}, bf16[192,1536]{1,0:T(8,128)(2,1)S(1)}, u32[]{:S(2)}, u32[]{:S(2)}) %collective-permute-start.5) | collective-permute-done | bytes 589856 | tf_op jit(solution)/shard_map/ppermute | solution.py:110
  71.8 2.4 slice_reduce_fusion.48
  74.2 1.9 slice_reduce_fusion.46
  76.2 0.0 copy-start.99
  76.3 1.6 slice_reduce_fusion.47
  78.1 0.0 copy-start.4
  78.1 0.0 copy-start.6
  78.1 1.2 select_maximum_fusion.2
  79.4 6.0 %collective-permute-done.6 = bf16[192,1536]{1,0:T(8,128)(2,1)} collective-permute-done((bf16[192,1536]{1,0:T(8,128)(2,1)S(1)}, bf16[192,1536]{1,0:T(8,128)(2,1)}, u32[]{:S(2)}, u32[]{:S(2)}) %collective-permute-start.6) | collective-permute-done | bytes 589856 | tf_op jit(solution)/shard_map/ppermute | solution.py:110
  85.6 0.0 copy-start.10
  85.6 0.0 copy-start.98
  85.6 3.4 fusion.166
  89.3 0.2 multiply_reduce_fusion.2
  89.5 8.7 %collective-permute-done.7 = bf16[192,1536]{1,0:T(8,128)(2,1)S(1)} collective-permute-done((bf16[192,1536]{1,0:T(8,128)(2,1)}, bf16[192,1536]{1,0:T(8,128)(2,1)S(1)}, u32[]{:S(2)}, u32[]{:S(2)}) %collective-permute-start.7) | collective-permute-done | bytes 589856 | tf_op jit(solution)/shard_map/ppermute | solution.py:110
  98.2 0.1 add_convert_fusion.1
  98.4 12.4 %all_gather.3 = bf16[12,16,1536]{2,1,0:T(8,128)(2,1)S(1)} all-gather(bf16[3,16,1536]{2,1,0:T(8,128)(2,1)S(1)} %add_convert_fusion.1), channel_id=1, replica_groups=mesh['fsdp'=8,'rows'=4] {'rows'}, dimensions={0}, use_global_device_ids=true | all-gather | bytes 737280 | tf_op jit(solution)/shard_map/all_gather | solution.py:119
  110.8 0.0 copy-start.2
  110.9 1.2 constant_dynamic-update-slice_fusion.13
  112.1 0.0 copy-done.2
  112.2 0.0 copy-start
  112.3 1.0 copy-done
  113.4 1.1 constant_dynamic-update-slice_fusion.5
  114.6 0.0 copy-start.8
  114.7 0.0 copy-start.100
  114.8 1.0 copy-done.8
  115.8 5.2 %fusion.15 = (f32[1536]{0:T(1024)S(1)}, f32[1536]{0:T(1024)S(1)}, f32[192,1536]{1,0:T(8,128)S(1)}, f32[192,1536]{1,0:T(8,128)}) fusion(bf16[1,12,16,1536]{3,2,1,0:T(8,128)(2,1)S(1)} %copy-done.8, f32[1536]{0:T(1024)S(1)} %copy-done.100, bf16[192,1536]{1,0:T(8,128)(2,1)S(1)} %bitcast.20, bf16[3072,1536]{1,0:T(8,128)(2,1)S(1)} %constant_dynamic-update-slice_fusion, ...), kind=kOutput, calls=%fused_computation.68 | convolution fusion | flops 926610432 | bytes 8278020 | tf_op jit(solution)/shard_map/dot_general | solution.py:123
  121.0 0.6 copy-done.94
  121.6 0.6 multiply_reduce_fusion.3
  122.2 11.6 %all-reduce.2 = (f32[]{:T(128)}, f32[]{:T(128)}) all-reduce(f32[]{:T(128)} %get-tuple-element.115, f32[]{:T(128)} %get-tuple-element.114), channel_id=1, replica_groups=mesh['fsdp'=8,'rows'=4] {'rows'}, use_global_device_ids=true, to_apply=%region_4.5 | all-reduce | flops 2 | bytes 16 | tf_op jit(solution)/shard_map/psum | solution.py:128
  135.1 0.7 multiply_add_fusion
  135.8 3.1 fusion.14
  138.9 4.9 %fusion.8 = bf16[12,16,1536]{2,1,0:T(8,128)(2,1)} fusion(bf16[12,16,1536]{2,1,0:T(8,128)(2,1)S(1)} %bitcast.22, bf16[3072,1536]{1,0:T(8,128)(2,1)} %copy-done.93, s32[]{:T(128)S(6)} %select_n.14), kind=kOutput, calls=%fused_computation.57 | convolution fusion | flops 906264576 | bytes 5898244 | tf_op jit(solution)/shard_map/hwf,cf->hwc/dot_general | solution.py:144
  143.8 0.0 reduce-scatter.3.cloned.1.call-update
  143.8 0.0 reduce-scatter.5.cloned.1.call-start
  143.9 3.6 convolution_convert_fusion
  147.4 0.0 reduce-scatter.5.cloned.1.call-update
  147.5 0.2 all-reduce.5.cloned.1.call-start
  147.7 14.8 %reduce-scatter.3.cloned.1.call-done = bf16[3,16,1536]{2,1,0:T(8,128)(2,1)} async-done(((bf16[12,16,1536]{2,1,0:T(8,128)(2,1)}), bf16[3,16,1536]{2,1,0:T(8,128)(2,1)}) %reduce-scatter.3.cloned.1.call-update) | async-done | bytes 147472 | tf_op jit(solution)/shard_map/reduce_scatter | solution.py:143
  162.5 1.1 fusion.153
  163.6 1.9 fusion.151
  165.5 0.0 copy-start.5
  165.5 0.0 copy-start.7
  165.5 2.7 collective-permute-start.10
  168.2 3.0 collective-permute-start.9
  171.2 0.8 fusion.152
  172.0 0.6 fusion.142
  173.2 0.5 stack.199
  174.2 0.8 reshape.62
  174.9 0.0 all-reduce.5.cloned.1.call-update
  175.0 0.2 select_maximum_fusion
  175.6 2.8 fusion.159
  178.4 83.4 %reduce-scatter.5.cloned.1.call-done = bf16[192,1536]{1,0:T(8,128)(2,1)} async-done(((bf16[1536,1536]{1,0:T(8,128)(2,1)}), bf16[192,1536]{1,0:T(8,128)(2,1)}) %reduce-scatter.5.cloned.1.call-update) | async-done | bytes 589840 | tf_op jit(solution)/shard_map/reduce_scatter | solution.py:139
  261.8 2.2 convert_element_type.489
  264.0 130.4 %all-reduce.5.cloned.1.call-done = f32[7,7,1536]{2,1,0:T(8,128)} async-done(((f32[7,7,1536]{2,1,0:T(8,128)}), f32[7,7,1536]{2,1,0:T(8,128)}) %all-reduce.5.cloned.1.call-update) | async-done | bytes 301072 | tf_op jit(solution)/shard_map/psum | solution.py:157
  394.3 1.7 copy.30
  (262 shorter events, 1.3 us)
Async XLA Ops:
  7.2 78.2 %copy-start.3 = (bf16[1,3,16,1536]{3,2,1,0:T(8,128)(2,1)S(1)}, bf16[1,3,16,1536]{3,2,1,0:T(8,128)(2,1)}, u32[]{:S(2)}) copy-start(bf16[1,3,16,1536]{3,2,1,0:T(8,128)(2,1)} %param.10) | copy-start | bytes 442372
  7.2 155.3 %reduce-scatter.3.cloned.1.call-start = ((), (), s32[]{:S(2)}) async-start(), calls=%async_computation.2 | async-start | bytes 737280 | tf_op jit(solution)/shard_map/reduce_scatter | solution.py:143
  7.2 18.4 %collective-permute-start.2 = (bf16[192,1536]{1,0:T(8,128)(2,1)}, bf16[192,1536]{1,0:T(8,128)(2,1)S(1)}, u32[]{:S(2)}, u32[]{:S(2)}) collective-permute-start(bf16[192,1536]{1,0:T(8,128)(2,1)} %param.15), channel_id=1, source_target_pairs={{0,4},{4,8},{8,12},{12,16},{16,20},{20,24},{24,28},{28,0},{1,5},{5... | collective-permute-start | bytes 1769480 | tf_op jit(solution)/shard_map/ppermute | solution.py:110
  25.6 16.3 %collective-permute-start.3 = (bf16[192,1536]{1,0:T(8,128)(2,1)S(1)}, bf16[192,1536]{1,0:T(8,128)(2,1)S(1)}, u32[]{:S(2)}, u32[]{:S(2)}) collective-permute-start(bf16[192,1536]{1,0:T(8,128)(2,1)S(1)} %collective-permute-done.2), channel_id=1, source_target_pairs={{0,4},{4,8},{8,12},{12,16},{16,20},{20,24},{24,28},{28,0},{1,5},{5... | collective-permute-start | bytes 1769480 | tf_op jit(solution)/shard_map/ppermute | solution.py:110
  41.9 15.4 %collective-permute-start.4 = (bf16[192,1536]{1,0:T(8,128)(2,1)S(1)}, bf16[192,1536]{1,0:T(8,128)(2,1)S(1)}, u32[]{:S(2)}, u32[]{:S(2)}) collective-permute-start(bf16[192,1536]{1,0:T(8,128)(2,1)S(1)} %collective-permute-done.3), channel_id=1, source_target_pairs={{0,4},{4,8},{8,12},{12,16},{16,20},{20,24},{24,28},{28,0},{1,5},{5... | collective-permute-start | bytes 1769480 | tf_op jit(solution)/shard_map/ppermute | solution.py:110
  57.3 14.4 %collective-permute-start.5 = (bf16[192,1536]{1,0:T(8,128)(2,1)S(1)}, bf16[192,1536]{1,0:T(8,128)(2,1)S(1)}, u32[]{:S(2)}, u32[]{:S(2)}) collective-permute-start(bf16[192,1536]{1,0:T(8,128)(2,1)S(1)} %collective-permute-done.4), channel_id=1, source_target_pairs={{0,4},{4,8},{8,12},{12,16},{16,20},{20,24},{24,28},{28,0},{1,5},{5... | collective-permute-start | bytes 1769480 | tf_op jit(solution)/shard_map/ppermute | solution.py:110
  57.3 20.8 %collective-permute-start = (bf16[3,16,1536]{2,1,0:T(8,128)(2,1)}, bf16[3,16,1536]{2,1,0:T(8,128)(2,1)S(1)}, u32[]{:S(2)}, u32[]{:S(2)}) collective-permute-start(bf16[3,16,1536]{2,1,0:T(8,128)(2,1)} %bitcast.23), channel_id=1, source_target_pairs={{0,1},{1,2},{2,3},{4,5},{5,6},{6,7},{8,9},{9,10},{10,11},{12,13},{... | collective-permute-start | bytes 442376 | tf_op jit(solution)/shard_map/ppermute | solution.py:14
  63.0 15.1 %collective-permute-start.1 = (bf16[3,16,1536]{2,1,0:T(8,128)(2,1)}, bf16[3,16,1536]{2,1,0:T(8,128)(2,1)S(1)}, u32[]{:S(2)}, u32[]{:S(2)}) collective-permute-start(bf16[3,16,1536]{2,1,0:T(8,128)(2,1)} %bitcast.24), channel_id=1, source_target_pairs={{1,0},{2,1},{3,2},{5,4},{6,5},{7,6},{9,8},{10,9},{11,10},{13,12},{... | collective-permute-start | bytes 442376 | tf_op jit(solution)/shard_map/ppermute | solution.py:17
  71.8 13.6 %copy-start.1 = (bf16[192,1536]{1,0:T(8,128)(2,1)}, bf16[192,1536]{1,0:T(8,128)(2,1)S(1)}, u32[]{:S(2)}) copy-start(bf16[192,1536]{1,0:T(8,128)(2,1)S(1)} %collective-permute-done.5) | copy-start | bytes 1769476
  71.8 13.6 %collective-permute-start.6 = (bf16[192,1536]{1,0:T(8,128)(2,1)S(1)}, bf16[192,1536]{1,0:T(8,128)(2,1)}, u32[]{:S(2)}, u32[]{:S(2)}) collective-permute-start(bf16[192,1536]{1,0:T(8,128)(2,1)S(1)} %collective-permute-done.5), channel_id=1, source_target_pairs={{0,4},{4,8},{8,12},{12,16},{16,20},{20,24},{24,28},{28,0},{1,5},{5... | collective-permute-start | bytes 1769480 | tf_op jit(solution)/shard_map/ppermute | solution.py:110
  74.2 14.9 %copy-start.11 = (f32[1536]{0:T(1024)}, f32[1536]{0:T(1024)S(1)}, u32[]{:S(2)}) copy-start(f32[1536]{0:T(1024)S(1)} %get-tuple-element.61) | copy-start | bytes 18436
  76.1 9.3 %copy-start.13 = (f32[1536]{0:T(1024)S(1)}, f32[1536]{0:T(1024)}, u32[]{:S(2)}) copy-start(f32[1536]{0:T(1024)} %get-tuple-element.62) | copy-start | bytes 18436
  76.1 9.3 %copy-start.15 = (f32[1536]{0:T(1024)S(1)}, f32[1536]{0:T(1024)}, u32[]{:S(2)}) copy-start(f32[1536]{0:T(1024)} %get-tuple-element.63) | copy-start | bytes 18436
  76.1 9.3 %copy-start.17 = (f32[1536]{0:T(1024)S(1)}, f32[1536]{0:T(1024)}, u32[]{:S(2)}) copy-start(f32[1536]{0:T(1024)} %get-tuple-element.64) | copy-start | bytes 18436
  76.1 9.3 %copy-start.19 = (f32[1536]{0:T(1024)S(1)}, f32[1536]{0:T(1024)}, u32[]{:S(2)}) copy-start(f32[1536]{0:T(1024)} %get-tuple-element.65) | copy-start | bytes 18436
  76.1 9.3 %copy-start.21 = (f32[1536]{0:T(1024)S(1)}, f32[1536]{0:T(1024)}, u32[]{:S(2)}) copy-start(f32[1536]{0:T(1024)} %get-tuple-element.66) | copy-start | bytes 18436
  76.1 9.3 %copy-start.23 = (f32[1536]{0:T(1024)S(1)}, f32[1536]{0:T(1024)}, u32[]{:S(2)}) copy-start(f32[1536]{0:T(1024)} %get-tuple-element.67) | copy-start | bytes 18436
  76.1 9.3 %copy-start.25 = (f32[1536]{0:T(1024)S(1)}, f32[1536]{0:T(1024)}, u32[]{:S(2)}) copy-start(f32[1536]{0:T(1024)} %get-tuple-element.68) | copy-start | bytes 18436
  76.1 9.3 %copy-start.27 = (f32[1536]{0:T(1024)S(1)}, f32[1536]{0:T(1024)}, u32[]{:S(2)}) copy-start(f32[1536]{0:T(1024)} %get-tuple-element.69) | copy-start | bytes 18436
  76.1 9.3 %copy-start.29 = (f32[1536]{0:T(1024)S(1)}, f32[1536]{0:T(1024)}, u32[]{:S(2)}) copy-start(f32[1536]{0:T(1024)} %get-tuple-element.70) | copy-start | bytes 18436
  76.1 9.3 %copy-start.31 = (f32[1536]{0:T(1024)S(1)}, f32[1536]{0:T(1024)}, u32[]{:S(2)}) copy-start(f32[1536]{0:T(1024)} %get-tuple-element.90) | copy-start | bytes 18436
  76.2 9.3 %copy-start.33 = (f32[1536]{0:T(1024)S(1)}, f32[1536]{0:T(1024)}, u32[]{:S(2)}) copy-start(f32[1536]{0:T(1024)} %get-tuple-element.91) | copy-start | bytes 18436
  76.2 9.3 %copy-start.35 = (f32[1536]{0:T(1024)S(1)}, f32[1536]{0:T(1024)}, u32[]{:S(2)}) copy-start(f32[1536]{0:T(1024)} %get-tuple-element.92) | copy-start | bytes 18436
  76.2 9.3 %copy-start.37 = (f32[1536]{0:T(1024)S(1)}, f32[1536]{0:T(1024)}, u32[]{:S(2)}) copy-start(f32[1536]{0:T(1024)} %get-tuple-element.93) | copy-start | bytes 18436
  76.2 9.3 %copy-start.39 = (f32[1536]{0:T(1024)S(1)}, f32[1536]{0:T(1024)}, u32[]{:S(2)}) copy-start(f32[1536]{0:T(1024)} %get-tuple-element.94) | copy-start | bytes 18436
  76.2 9.3 %copy-start.41 = (f32[1536]{0:T(1024)S(1)}, f32[1536]{0:T(1024)}, u32[]{:S(2)}) copy-start(f32[1536]{0:T(1024)} %get-tuple-element.95) | copy-start | bytes 18436
  76.2 9.3 %copy-start.43 = (f32[1536]{0:T(1024)S(1)}, f32[1536]{0:T(1024)}, u32[]{:S(2)}) copy-start(f32[1536]{0:T(1024)} %get-tuple-element.96) | copy-start | bytes 18436
  76.2 9.3 %copy-start.45 = (f32[1536]{0:T(1024)S(1)}, f32[1536]{0:T(1024)}, u32[]{:S(2)}) copy-start(f32[1536]{0:T(1024)} %get-tuple-element.97) | copy-start | bytes 18436
  76.2 9.3 %copy-start.47 = (f32[1536]{0:T(1024)S(1)}, f32[1536]{0:T(1024)}, u32[]{:S(2)}) copy-start(f32[1536]{0:T(1024)} %get-tuple-element.98) | copy-start | bytes 18436
  76.2 9.3 %copy-start.49 = (f32[1536]{0:T(1024)S(1)}, f32[1536]{0:T(1024)}, u32[]{:S(2)}) copy-start(f32[1536]{0:T(1024)} %get-tuple-element.99) | copy-start | bytes 18436
  76.2 9.3 %copy-start.51 = (f32[1536]{0:T(1024)S(1)}, f32[1536]{0:T(1024)}, u32[]{:S(2)}) copy-start(f32[1536]{0:T(1024)} %get-tuple-element.100) | copy-start | bytes 18436
  76.2 9.3 %copy-start.99 = (f32[1536]{0:T(1024)S(1)}, f32[1536]{0:T(1024)}, u32[]{:S(2)}) copy-start(f32[1536]{0:T(1024)} %param.12) | copy-start | bytes 18436
  77.9 11.2 %copy-start.53 = (f32[1536]{0:T(1024)}, f32[1536]{0:T(1024)S(1)}, u32[]{:S(2)}) copy-start(f32[1536]{0:T(1024)S(1)} %get-tuple-element.71) | copy-start | bytes 18436
  77.9 11.2 %copy-start.55 = (f32[1536]{0:T(1024)}, f32[1536]{0:T(1024)S(1)}, u32[]{:S(2)}) copy-start(f32[1536]{0:T(1024)S(1)} %get-tuple-element.72) | copy-start | bytes 18436
  77.9 11.2 %copy-start.57 = (f32[1536]{0:T(1024)}, f32[1536]{0:T(1024)S(1)}, u32[]{:S(2)}) copy-start(f32[1536]{0:T(1024)S(1)} %get-tuple-element.73) | copy-start | bytes 18436
  77.9 11.1 %copy-start.59 = (f32[1536]{0:T(1024)}, f32[1536]{0:T(1024)S(1)}, u32[]{:S(2)}) copy-start(f32[1536]{0:T(1024)S(1)} %get-tuple-element.74) | copy-start | bytes 18436
  77.9 11.1 %copy-start.61 = (f32[1536]{0:T(1024)}, f32[1536]{0:T(1024)S(1)}, u32[]{:S(2)}) copy-start(f32[1536]{0:T(1024)S(1)} %get-tuple-element.75) | copy-start | bytes 18436
  77.9 11.1 %copy-start.63 = (f32[1536]{0:T(1024)}, f32[1536]{0:T(1024)S(1)}, u32[]{:S(2)}) copy-start(f32[1536]{0:T(1024)S(1)} %get-tuple-element.76) | copy-start | bytes 18436
  78.0 11.1 %copy-start.65 = (f32[1536]{0:T(1024)}, f32[1536]{0:T(1024)S(1)}, u32[]{:S(2)}) copy-start(f32[1536]{0:T(1024)S(1)} %get-tuple-element.77) | copy-start | bytes 18436
  78.0 11.1 %copy-start.67 = (f32[1536]{0:T(1024)}, f32[1536]{0:T(1024)S(1)}, u32[]{:S(2)}) copy-start(f32[1536]{0:T(1024)S(1)} %get-tuple-element.78) | copy-start | bytes 18436
  78.0 11.1 %copy-start.69 = (f32[1536]{0:T(1024)}, f32[1536]{0:T(1024)S(1)}, u32[]{:S(2)}) copy-start(f32[1536]{0:T(1024)S(1)} %get-tuple-element.79) | copy-start | bytes 18436
  78.0 11.1 %copy-start.71 = (f32[1536]{0:T(1024)}, f32[1536]{0:T(1024)S(1)}, u32[]{:S(2)}) copy-start(f32[1536]{0:T(1024)S(1)} %get-tuple-element.80) | copy-start | bytes 18436
  78.0 11.1 %copy-start.73 = (f32[1536]{0:T(1024)}, f32[1536]{0:T(1024)S(1)}, u32[]{:S(2)}) copy-start(f32[1536]{0:T(1024)S(1)} %get-tuple-element.81) | copy-start | bytes 18436
  78.0 11.1 %copy-start.75 = (f32[1536]{0:T(1024)}, f32[1536]{0:T(1024)S(1)}, u32[]{:S(2)}) copy-start(f32[1536]{0:T(1024)S(1)} %get-tuple-element.82) | copy-start | bytes 18436
  78.0 11.1 %copy-start.77 = (f32[1536]{0:T(1024)}, f32[1536]{0:T(1024)S(1)}, u32[]{:S(2)}) copy-start(f32[1536]{0:T(1024)S(1)} %get-tuple-element.83) | copy-start | bytes 18436
  78.0 11.1 %copy-start.79 = (f32[1536]{0:T(1024)}, f32[1536]{0:T(1024)S(1)}, u32[]{:S(2)}) copy-start(f32[1536]{0:T(1024)S(1)} %get-tuple-element.84) | copy-start | bytes 18436
  78.0 11.1 %copy-start.81 = (f32[1536]{0:T(1024)}, f32[1536]{0:T(1024)S(1)}, u32[]{:S(2)}) copy-start(f32[1536]{0:T(1024)S(1)} %get-tuple-element.85) | copy-start | bytes 18436
  78.0 11.1 %copy-start.83 = (f32[1536]{0:T(1024)}, f32[1536]{0:T(1024)S(1)}, u32[]{:S(2)}) copy-start(f32[1536]{0:T(1024)S(1)} %get-tuple-element.86) | copy-start | bytes 18436
  78.1 11.1 %copy-start.85 = (f32[1536]{0:T(1024)}, f32[1536]{0:T(1024)S(1)}, u32[]{:S(2)}) copy-start(f32[1536]{0:T(1024)S(1)} %get-tuple-element.87) | copy-start | bytes 18436
  78.1 11.1 %copy-start.87 = (f32[1536]{0:T(1024)}, f32[1536]{0:T(1024)S(1)}, u32[]{:S(2)}) copy-start(f32[1536]{0:T(1024)S(1)} %get-tuple-element.88) | copy-start | bytes 18436
  78.1 11.1 %copy-start.89 = (f32[1536]{0:T(1024)}, f32[1536]{0:T(1024)S(1)}, u32[]{:S(2)}) copy-start(f32[1536]{0:T(1024)S(1)} %get-tuple-element.89) | copy-start | bytes 18436
  78.1 11.1 %copy-start.4 = (bf16[3,16,1536]{2,1,0:T(8,128)(2,1)}, bf16[3,16,1536]{2,1,0:T(8,128)(2,1)S(1)}, u32[]{:S(2)}) copy-start(bf16[3,16,1536]{2,1,0:T(8,128)(2,1)S(1)} %collective-permute-done) | copy-start | bytes 442372
  78.1 11.1 %copy-start.6 = (bf16[3,16,1536]{2,1,0:T(8,128)(2,1)}, bf16[3,16,1536]{2,1,0:T(8,128)(2,1)S(1)}, u32[]{:S(2)}) copy-start(bf16[3,16,1536]{2,1,0:T(8,128)(2,1)S(1)} %collective-permute-done.1) | copy-start | bytes 442372
  85.4 12.8 %collective-permute-start.7 = (bf16[192,1536]{1,0:T(8,128)(2,1)}, bf16[192,1536]{1,0:T(8,128)(2,1)S(1)}, u32[]{:S(2)}, u32[]{:S(2)}) collective-permute-start(bf16[192,1536]{1,0:T(8,128)(2,1)} %collective-permute-done.6), channel_id=1, source_target_pairs={{0,4},{4,8},{8,12},{12,16},{16,20},{20,24},{24,28},{28,0},{1,5},{5... | collective-permute-start | bytes 1769480 | tf_op jit(solution)/shard_map/ppermute | solution.py:110
  85.6 12.6 %copy-start.10 = (f32[1536]{0:T(1024)S(1)}, f32[1536]{0:T(1024)}, u32[]{:S(2)}) copy-start(f32[1536]{0:T(1024)} %param.13) | copy-start | bytes 18436
  85.6 12.6 %copy-start.98 = (f32[1536]{0:T(1024)S(1)}, f32[1536]{0:T(1024)}, u32[]{:S(2)}) copy-start(f32[1536]{0:T(1024)} %param.14) | copy-start | bytes 18436
  89.3 8.9 %copy-start.91 = (f32[3,16]{1,0:T(4,128)}, f32[3,16]{1,0:T(4,128)S(1)}, u32[]{:S(2)}) copy-start(f32[3,16]{1,0:T(4,128)S(1)} %broadcast_multiply_fusion.2) | copy-start | bytes 580
  98.2 12.6 %collective-permute-start.8 = (bf16[192,1536]{1,0:T(8,128)(2,1)S(1)}, bf16[192,1536]{1,0:T(8,128)(2,1)S(1)}, u32[]{:S(2)}, u32[]{:S(2)}) collective-permute-start(bf16[192,1536]{1,0:T(8,128)(2,1)S(1)} %collective-permute-done.7), channel_id=1, source_target_pairs={{0,4},{4,8},{8,12},{12,16},{16,20},{20,24},{24,28},{28,0},{1,5},{5... | collective-permute-start | bytes 1769480 | tf_op jit(solution)/shard_map/ppermute | solution.py:110
  143.8 118.0 %reduce-scatter.5.cloned.1.call-start = ((), (), s32[]{:S(2)}) async-start(), calls=%async_computation.3 | async-start | bytes 5308416 | tf_op jit(solution)/shard_map/reduce_scatter | solution.py:139
  147.4 15.1 %copy-start.92 = (f32[3,16]{1,0:T(4,128)S(1)}, f32[3,16]{1,0:T(4,128)}, u32[]{:S(2)}) copy-start(f32[3,16]{1,0:T(4,128)} %copy-done.91) | copy-start | bytes 580
  147.4 15.1 %copy-start.97 = (f32[3,16]{1,0:T(4,128)S(1)}, f32[3,16]{1,0:T(4,128)}, u32[]{:S(2)}) copy-start(f32[3,16]{1,0:T(4,128)} %copy-done.96) | copy-start | bytes 580
  147.5 246.9 %all-reduce.5.cloned.1.call-start = ((), (), s32[]{:S(2)}) async-start(), calls=%async_computation.4 | async-start | bytes 688128 | tf_op jit(solution)/shard_map/psum | solution.py:157
  165.5 9.5 %collective-permute-start.10 = (bf16[3,16,1536]{2,1,0:T(8,128)(2,1)S(1)}, bf16[3,16,1536]{2,1,0:T(8,128)(2,1)S(1)}, u32[]{:S(2)}, u32[]{:S(2)}) collective-permute-start(bf16[3,16,1536]{2,1,0:T(8,128)(2,1)S(1)} %get-tuple-element.118), channel_id=1, source_target_pairs={{1,0},{2,1},{3,2},{5,4},{6,5},{7,6},{9,8},{10,9},{11,10},{13,12},{... | collective-permute-start | bytes 442376 | tf_op jit(solution)/shard_map/ppermute | solution.py:17
  168.2 6.8 %collective-permute-start.9 = (bf16[3,16,1536]{2,1,0:T(8,128)(2,1)S(1)}, bf16[3,16,1536]{2,1,0:T(8,128)(2,1)S(1)}, u32[]{:S(2)}, u32[]{:S(2)}) collective-permute-start(bf16[3,16,1536]{2,1,0:T(8,128)(2,1)S(1)} %get-tuple-element.118), channel_id=1, source_target_pairs={{0,1},{1,2},{2,3},{4,5},{5,6},{6,7},{8,9},{9,10},{10,11},{12,13},{... | collective-permute-start | bytes 442376 | tf_op jit(solution)/shard_map/ppermute | solution.py:14
  (51 other events, 98.0 us)
Sparse Core Ops, SparseCore 0:
  143.9 18.5 reduce-scatter.2
  166.1 95.5 reduce-scatter.4
  267.7 126.6 all-reduce.4
